TPU v7x, 256 devices: a whole 4x4x8 slice. The times are simulated.
256 devices in a mesh: row: 16 (over y_hi, x, core), col: 16 (over z, y_lo).
Axes of the slice: x: 4, y: 4 (y_hi: 2, y_lo: 2; y = y_hi * 2 + y_lo), z: 8, core: 2. Of those that a mesh axis runs over, the one named last changes fastest.
Arguments:
- inputs: bfloat16 [1024, 16384], P('col', 'row'), may hold values from -6 to 6
- out_grad: bfloat16 [1024, 16384], P('col', 'row'), may hold values from -0.1875 to 0.1875
- states: bfloat16 [16384, 1024], P(('col', 'row')), may hold values from -6 to 6
- in_weight: bfloat16 [16384, 16384], P('row', 'col'), may hold values from -0.046875 to 0.046875
- out_weight: bfloat16 [16384, 16384], P('col', 'row'), may hold values from -0.046875 to 0.046875
- decay_rate: float32 [4, 16384], P(None, ('col', 'row')), may hold values from 0.0015625 to 0.1
- session_ids: int32 [4], replicated, may hold values from 0 to 3, each once
- lengths: int32 [4], replicated, may hold values from 1 to 256, 640 in all
Outputs:
- input_grad: bfloat16 [1024, 16384], P('col', 'row')
- in_weight_grad: bfloat16 [16384, 16384], P('row', 'col')
- out_weight_grad: bfloat16 [16384, 16384], P('col', 'row')
- rate_grad: float32 [4, 16384], P(None, ('col', 'row'))
Inputs may be any that keep to these rules, and one draw needn't show every extreme that they name: `session_ids`: each session appears in exactly one sequence. The lengths sum to 640.
All inputs are finite; a program needn't handle non-finite values.
Results may differ from a plain program's by a relative error of at most 0.024.
Values may be sent and summed in bfloat16 or wider, within the bound.
No kernel may reach another device: no remote copies, remote signals or barrier semaphores. Data moves between devices by JAX's collectives and lax.ppermute only.
A program may use at most 128 MiB of HBM per device.

v0:
```python
import jax
import jax.numpy as jnp
from jax import lax
from jax.sharding import PartitionSpec as P

exact_mode = lax.Precision.HIGHEST


def contract(left_side, right_side, left_dim, right_dim):
    return lax.dot_general(
        left_side,
        right_side,
        (((left_dim,), (right_dim,)), ((), ())),
        preferred_element_type=jnp.float32,
    )


def session_table(session_ids, table_rows):
    return (session_ids[:, None] == jnp.arange(table_rows, dtype=jnp.int32)[None, :]).astype(
        jnp.float32
    )


def adjoint_sweep(state_grad, rate_rows, onehot, seq_count):
    channels = state_grad.shape[0]
    seq_rate = jnp.dot(onehot, rate_rows, precision=exact_mode)
    decays = (1.0 - seq_rate).T
    grad_seq = state_grad.reshape(channels, seq_count, -1)
    factor = jnp.broadcast_to(decays[:, :, None], grad_seq.shape)

    def combine(suffix, current):
        return (suffix[0] * current[0], current[1] + current[0] * suffix[1])

    flipped = lax.associative_scan(combine, (jnp.flip(factor, 2), jnp.flip(grad_seq, 2)), axis=2)
    return jnp.flip(flipped[1], 2).reshape(channels, -1)


def rate_term(adjoint, states_share, onehot, seq_count):
    channels = adjoint.shape[0]
    adjoint_seq = adjoint.reshape(channels, seq_count, -1)
    previous = states_share.astype(jnp.float32).reshape(channels, seq_count, -1)
    per_seq = jnp.sum(adjoint_seq[:, :, 1:] * previous[:, :, :-1], axis=2)
    return -jnp.dot(onehot.T, per_seq.T, precision=exact_mode)


def per_device(inputs, out_grad, states, in_weight, out_weight, decay_rate, session_ids, lengths):
    seq_count = session_ids.shape[0]
    onehot = session_table(session_ids, decay_rate.shape[0])
    grad_rows, input_rows = (
        lax.all_gather(out_grad, "col", axis=0, tiled=True),
        lax.all_gather(inputs, "col", axis=0, tiled=True),
    )
    token_total = grad_rows.shape[0]
    bin_count = token_total // seq_count
    token_ids = jnp.arange(token_total, dtype=jnp.int32)
    seq_match = (token_ids // bin_count)[:, None] == jnp.arange(seq_count, dtype=jnp.int32)[None, :]
    seq_length = jnp.sum(jnp.where(seq_match, lengths[None, :], 0), axis=1)
    valid_bin = token_ids % bin_count >= bin_count - seq_length
    masked = jnp.where(valid_bin[:, None], grad_rows, jnp.zeros_like(grad_rows))
    out_weight_grad = jnp.dot(
        lax.all_gather(states, "row", axis=0, tiled=True),
        masked,
        preferred_element_type=jnp.float32,
    ).astype(jnp.bfloat16)
    state_grad = lax.psum_scatter(
        contract(out_weight, masked, 1, 1).astype(jnp.bfloat16),
        "row",
        scatter_dimension=0,
        tiled=True,
    ).astype(jnp.float32)
    adjoint = adjoint_sweep(state_grad, decay_rate, onehot, seq_count)
    rate_grad = rate_term(adjoint, states, onehot, seq_count)
    gathered = lax.all_gather(adjoint.astype(jnp.bfloat16), "row", axis=0, tiled=True)
    in_weight_grad = contract(input_rows, gathered, 0, 1).astype(jnp.bfloat16)
    input_grad = lax.psum_scatter(
        contract(gathered, in_weight, 0, 1).astype(jnp.bfloat16),
        "col",
        scatter_dimension=0,
        tiled=True,
    )
    return (input_grad, in_weight_grad, out_weight_grad, rate_grad)


def solution(mesh):
    return jax.shard_map(
        per_device,
        mesh=mesh,
        in_specs=(
            P("col", "row"),
            P("col", "row"),
            P(("col", "row"), None),
            P("row", "col"),
            P("col", "row"),
            P(None, ("col", "row")),
            P(),
            P(),
        ),
        out_specs=(P("col", "row"), P("row", "col"), P("col", "row"), P(None, ("col", "row"))),
        check_vma=False,
    )
```

profile of v0, /device:TPU:2, one launch (start us, length us, event | category | flops | bytes accessed | tf_op | source)
XLA Modules:
  0.0 521.6 jit_solution(5248064068096911527)
XLA Ops:
  8.7 76.5 %all-gather.5.cloned.1.call-done = bf16[1024,1024]{1,0:T(8,128)(2,1)} async-done(((bf16[64,1024]{1,0:T(8,128)(2,1)}), bf16[1024,1024]{1,0:T(8,128)(2,1)}) %all-gather.5.cloned.1.call-update) | async-done | bytes 2097168 | tf_op jit(solution)/shard_map/all_gather | solution.py:50
  85.2 5.3 %convert_bitcast_fusion.2 = bf16[1024,1024]{0,1:T(8,128)(2,1)} fusion(bf16[1024,1024]{1,0:T(8,128)(2,1)S(1)} %copy-done, bf16[1024,1024]{1,0:T(8,128)(2,1)} %all-gather.5.cloned.1.call-done, pred[1024]{0:T(1024)(128)(4,1)S(1)} %fusion.9), kind=kOutput, calls=%fused_computation.2 | convolution fusion | flops 2149580800 | bytes 6292480 | tf_op jit(solution)/shard_map/dot_general | solution.py:10
  90.5 3.9 copy.78
  95.8 75.4 %reduce-scatter.7.cloned.1.call-done = bf16[64,1024]{1,0:T(8,128)(2,1)} async-done(((bf16[1024,1024]{1,0:T(8,128)(2,1)}), bf16[64,1024]{1,0:T(8,128)(2,1)}) %reduce-scatter.7.cloned.1.call-update) | async-done | bytes 131088
  171.1 1.1 copy.79
  173.7 2.2 slice.229
  175.9 2.2 slice.225
  178.1 2.8 slice.223
  181.0 2.2 slice.226
  183.2 2.2 slice.224
  185.5 1.1 slice.236
  186.6 1.2 slice.232
  187.7 1.8 slice.230
  189.5 1.3 slice.233
  190.8 1.2 slice.231
  193.2 1.2 slice.237
  195.1 1.3 slice.238
  196.3 0.9 fusion.22
  197.9 1.0 slice.244
  198.9 1.0 slice.247
  199.9 1.0 slice.245
  200.8 1.0 fusion.21
  202.0 0.9 slice.253
  202.9 0.8 slice.251
  203.7 0.8 slice.254
  204.5 0.9 slice.252
  205.4 1.1 fusion.20
  207.4 0.8 slice.259
  208.9 1.0 multiply_add_fusion
  209.9 1.1 fusion.8
  211.1 0.9 fusion.19
  212.0 0.8 slice.249
  212.8 1.0 slice.242
  213.8 1.2 slice.235
  215.0 1.8 slice.228
  216.8 2.8 slice.222
  219.6 0.8 copy.81
  221.3 1.0 copy.85
  222.3 1.0 copy.86
  224.9 1.9 pad.54
  226.7 1.0 fusion.6
  228.9 2.0 pad.56
  230.9 0.9 fusion.5
  233.1 2.2 pad.58
  235.3 0.9 fusion.4
  236.3 0.8 pad.57
  237.2 1.4 pad.60
  238.5 1.0 fusion.3
  239.6 1.3 pad.59
  241.0 2.4 pad.62
  243.6 2.6 pad.61
  246.4 4.6 pad.63
  250.9 4.6 pad.64
  257.7 51.4 %all-gather.7.cloned.1.call-done = bf16[1024,1024]{1,0:T(8,128)(2,1)} async-done(((bf16[64,1024]{1,0:T(8,128)(2,1)}), bf16[1024,1024]{1,0:T(8,128)(2,1)}) %all-gather.7.cloned.1.call-update) | async-done | bytes 2097168 | tf_op jit(solution)/shard_map/all_gather | solution.py:73
  309.2 6.0 %convolution_convert_fusion = bf16[1024,1024]{1,0:T(8,128)(2,1)} fusion(bf16[1024,1024]{1,0:T(8,128)(2,1)} %all-gather.7.cloned.1.call-done, bf16[1024,1024]{1,0:T(8,128)(2,1)} %param.11), kind=kOutput, calls=%fused_computation.4 | convolution fusion | flops 2148532224 | bytes 6291456 | tf_op jit(solution)/shard_map/dot_general | solution.py:10
  315.2 0.9 copy-done.8
  316.1 47.9 %all-gather.11.cloned.1.call-done = bf16[1024,1024]{1,0:T(8,128)(2,1)} async-done(((bf16[64,1024]{1,0:T(8,128)(2,1)}), bf16[1024,1024]{1,0:T(8,128)(2,1)}) %all-gather.11.cloned.1.call-update) | async-done | bytes 2097168 | tf_op jit(solution)/shard_map/all_gather | solution.py:61
  364.1 6.2 %convert_bitcast_fusion = bf16[1024,1024]{0,1:T(8,128)(2,1)} fusion(bf16[1024,1024]{1,0:T(8,128)(2,1)} %all-gather.11.cloned.1.call-done, bf16[1024,1024]{1,0:T(8,128)(2,1)} %all-gather.5.cloned.1.call-done, pred[1024]{0:T(1024)(128)(4,1)S(1)} %fusion.9), kind=kOutput, calls=%fused_computation | convolution fusion | flops 2149580800 | bytes 6292480 | tf_op jit(solution)/shard_map/dot_general | solution.py:60
  370.3 3.9 copy.72
  374.7 0.8 convolution_negate_fusion
  375.6 61.5 %all-gather.9.cloned.1.call-done = bf16[1024,1024]{1,0:T(8,128)(2,1)} async-done(((bf16[64,1024]{1,0:T(8,128)(2,1)}), bf16[1024,1024]{1,0:T(8,128)(2,1)}) %all-gather.9.cloned.1.call-update) | async-done | bytes 2097168 | tf_op jit(solution)/shard_map/all_gather | solution.py:51
  437.1 5.9 %convert_bitcast_fusion.1 = bf16[1024,1024]{0,1:T(8,128)(2,1)} fusion(bf16[1024,1024]{1,0:T(8,128)(2,1)} %all-gather.7.cloned.1.call-done, bf16[1024,1024]{1,0:T(8,128)(2,1)} %all-gather.9.cloned.1.call-done), kind=kOutput, calls=%fused_computation.1 | convolution fusion | flops 2148532224 | bytes 6291456 | tf_op jit(solution)/shard_map/dot_general | solution.py:10
  443.0 3.9 copy.71
  446.9 67.6 %reduce-scatter.5.cloned.1.call-done = bf16[64,1024]{1,0:T(8,128)(2,1)} async-done(((bf16[1024,1024]{1,0:T(8,128)(2,1)}), bf16[64,1024]{1,0:T(8,128)(2,1)}) %reduce-scatter.5.cloned.1.call-update) | async-done | bytes 131088 | tf_op jit(solution)/shard_map/reduce_scatter | solution.py:75
  (95 shorter events, 16.8 us)
Async XLA Ops:
  7.2 78.1 %copy-start = (bf16[1024,1024]{1,0:T(8,128)(2,1)S(1)}, bf16[1024,1024]{1,0:T(8,128)(2,1)}, u32[]{:S(2)}) copy-start(bf16[1024,1024]{1,0:T(8,128)(2,1)} %param.12) | copy-start | bytes 6291460
  7.2 78.1 %all-gather.5.cloned.1.call-start = ((), (), s32[]{:S(2)}) async-start(), calls=%async_computation.2 | async-start | bytes 2228224 | tf_op jit(solution)/shard_map/all_gather | solution.py:50
  7.9 163.2 %reduce-scatter.7.cloned.1.call-start = ((), (), s32[]{:S(2)}) async-start(), calls=%async_computation.7 | async-start | bytes 2228224
  94.5 0.7 copy-start.10
  94.5 0.7 copy-start.11
  94.5 214.7 %all-gather.7.cloned.1.call-start = ((), (), s32[]{:S(2)}) async-start(), calls=%async_computation.3 | async-start | bytes 2228224 | tf_op jit(solution)/shard_map/all_gather | solution.py:73
  212.0 11.3 %copy-start.9 = (f32[64,4,1]{2,0,1:T(8,128)S(1)}, f32[64,4,1]{2,0,1:T(8,128)}, u32[]{:S(2)}) copy-start(f32[64,4,1]{2,0,1:T(8,128)} %get-tuple-element.48) | copy-start | bytes 3076
  220.5 10.4 %copy-start.4 = (f32[64,4,7]{2,0,1:T(8,128)S(1)}, f32[64,4,7]{2,0,1:T(8,128)}, u32[]{:S(2)}) copy-start(f32[64,4,7]{2,0,1:T(8,128)} %slice.244) | copy-start | bytes 21508
  224.9 10.4 %copy-start.3 = (f32[64,4,15]{2,0,1:T(8,128)S(1)}, f32[64,4,15]{2,0,1:T(8,128)}, u32[]{:S(2)}) copy-start(f32[64,4,15]{2,0,1:T(8,128)} %slice.237) | copy-start | bytes 46084
  228.9 9.6 %copy-start.2 = (f32[64,4,31]{2,0,1:T(8,128)S(1)}, f32[64,4,31]{2,0,1:T(8,128)}, u32[]{:S(2)}) copy-start(f32[64,4,31]{2,0,1:T(8,128)} %slice.230) | copy-start | bytes 95236
  233.1 10.3 %copy-start.1 = (f32[64,4,63]{2,0,1:T(8,128)S(1)}, f32[64,4,63]{2,0,1:T(8,128)}, u32[]{:S(2)}) copy-start(f32[64,4,63]{2,0,1:T(8,128)} %slice.223) | copy-start | bytes 193540
  233.1 10.3 %copy-start.7 = (f32[64,4,63]{2,0,1:T(8,128)S(1)}, f32[64,4,63]{2,0,1:T(8,128)}, u32[]{:S(2)}) copy-start(f32[64,4,63]{2,0,1:T(8,128)} %slice.222) | copy-start | bytes 193540
  237.1 9.1 %copy-start.6 = (f32[64,4,127]{2,0,1:T(8,128)S(1)}, f32[64,4,127]{2,0,1:T(8,128)}, u32[]{:S(2)}) copy-start(f32[64,4,127]{2,0,1:T(8,128)} %slice.212) | copy-start | bytes 390148
  238.5 7.7 %copy-start.5 = (f32[64,4,1]{2,0,1:T(8,128)S(1)}, f32[64,4,1]{2,0,1:T(8,128)}, u32[]{:S(2)}) copy-start(f32[64,4,1]{2,0,1:T(8,128)} %copy.81) | copy-start | bytes 3076
  256.5 107.5 %all-gather.11.cloned.1.call-start = ((), (), s32[]{:S(2)}) async-start(), calls=%async_computation.6 | async-start | bytes 2228224 | tf_op jit(solution)/shard_map/all_gather | solution.py:61
  257.1 180.0 %all-gather.9.cloned.1.call-start = ((), (), s32[]{:S(2)}) async-start(), calls=%async_computation.5 | async-start | bytes 2228224 | tf_op jit(solution)/shard_map/all_gather | solution.py:51
  257.7 256.8 %reduce-scatter.5.cloned.1.call-start = ((), (), s32[]{:S(2)}) async-start(), calls=%async_computation.4 | async-start | bytes 2228224 | tf_op jit(solution)/shard_map/reduce_scatter | solution.py:75
  315.1 0.9 copy-start.8
Sparse Core Ops, SparseCore 0:
  9.8 75.4 all-gather.4
  94.6 76.4 reduce-scatter.6
  256.6 52.4 all-gather.6
  311.7 52.2 all-gather.10
  365.7 71.3 all-gather.8
  440.1 74.4 reduce-scatter.4
where the time goes:
time: 525 us; the launch traced here: 522 us
  waiting for transfers between devices  382 us (73%)
  local copies, waits for them, and re-layouts  86.1 us (16%)
  matrix products  24.4 us (5%)
  between operations  14.9 us (3%)
  other arithmetic  13.8 us (3%)
    unnamed x7, waiting for transfers between devices  77.2 us
    all_gather x1, waiting for transfers between devices, per_device(): lax.all_gather(out_grad, 'col', axis=0, tiled=True)  76.5 us
    reduce_scatter x1, waiting for transfers between devices, per_device(): lax.psum_scatter(contract(gathered, in_weight, 0, 1).astype(jnp.bfloat16)...  67.6 us
    all_gather x1, waiting for transfers between devices, per_device(): lax.all_gather(inputs, 'col', axis=0, tiled=True)  61.5 us
    all_gather x1, waiting for transfers between devices, per_device(): lax.all_gather(adjoint.astype(jnp.bfloat16), 'row', axis=0, tiled=True)  51.4 us
    all_gather x1, waiting for transfers between devices, per_device(): lax.all_gather(states, 'row', axis=0, tiled=True)  47.9 us
    slice x45, local copies, waits for them, and re-layouts, adjoint_sweep(): lax.associative_scan(combine, (jnp.flip(factor, 2), jnp.flip(grad_seq, 2)...  42 us
    pad x14, local copies, waits for them, and re-layouts, adjoint_sweep(): lax.associative_scan(combine, (jnp.flip(factor, 2), jnp.flip(grad_seq, 2)...  25.1 us
  transfers between devices with their start and end apart: 6, of which 6 were waited for; matrix products, arithmetic and copies ran while one was open for 5% of the time, Pallas kernels for 0%

commit v1 on v0

--- a/solution.py
+++ b/solution.py
@@ -21,18 +21,32 @@
     )
 
 
+def gather_rows(share, axis_name, parts):
+    spread = jnp.broadcast_to(share[None], (parts,) + share.shape)
+    return lax.all_to_all(spread, axis_name, 0, 0).reshape((-1,) + share.shape[1:])
+
+
+def scatter_sum(partial, axis_name, parts):
+    pieces = lax.all_to_all(partial.reshape((parts, -1) + partial.shape[1:]), axis_name, 0, 0)
+    return jnp.sum(pieces.astype(jnp.float32), axis=0)
+
+
 def adjoint_sweep(state_grad, rate_rows, onehot, seq_count):
     channels = state_grad.shape[0]
     seq_rate = jnp.dot(onehot, rate_rows, precision=exact_mode)
     decays = (1.0 - seq_rate).T
-    grad_seq = state_grad.reshape(channels, seq_count, -1)
-    factor = jnp.broadcast_to(decays[:, :, None], grad_seq.shape)
-
-    def combine(suffix, current):
-        return (suffix[0] * current[0], current[1] + current[0] * suffix[1])
-
-    flipped = lax.associative_scan(combine, (jnp.flip(factor, 2), jnp.flip(grad_seq, 2)), axis=2)
-    return jnp.flip(flipped[1], 2).reshape(channels, -1)
+    running = state_grad.reshape(channels, seq_count, -1)
+    bins = running.shape[2]
+    factor = decays[:, :, None]
+    shift = 1
+    while shift < bins:
+        ahead = jnp.concatenate(
+            [running[:, :, shift:], jnp.zeros((channels, seq_count, shift), running.dtype)], axis=2
+        )
+        running = running + factor * ahead
+        factor = factor * factor
+        shift *= 2
+    return running.reshape(channels, -1)
 
 
 def rate_term(adjoint, states_share, onehot, seq_count):
@@ -44,12 +58,11 @@
 
 
 def per_device(inputs, out_grad, states, in_weight, out_weight, decay_rate, session_ids, lengths):
+    n_row = lax.axis_size("row")
+    n_col = lax.axis_size("col")
     seq_count = session_ids.shape[0]
     onehot = session_table(session_ids, decay_rate.shape[0])
-    grad_rows, input_rows = (
-        lax.all_gather(out_grad, "col", axis=0, tiled=True),
-        lax.all_gather(inputs, "col", axis=0, tiled=True),
-    )
+    grad_rows = gather_rows(out_grad, "col", n_col)
     token_total = grad_rows.shape[0]
     bin_count = token_total // seq_count
     token_ids = jnp.arange(token_total, dtype=jnp.int32)
@@ -57,27 +70,19 @@
     seq_length = jnp.sum(jnp.where(seq_match, lengths[None, :], 0), axis=1)
     valid_bin = token_ids % bin_count >= bin_count - seq_length
     masked = jnp.where(valid_bin[:, None], grad_rows, jnp.zeros_like(grad_rows))
-    out_weight_grad = jnp.dot(
-        lax.all_gather(states, "row", axis=0, tiled=True),
-        masked,
-        preferred_element_type=jnp.float32,
-    ).astype(jnp.bfloat16)
-    state_grad = lax.psum_scatter(
-        contract(out_weight, masked, 1, 1).astype(jnp.bfloat16),
-        "row",
-        scatter_dimension=0,
-        tiled=True,
-    ).astype(jnp.float32)
+    state_grad = scatter_sum(contract(out_weight, masked, 1, 1).astype(jnp.bfloat16), "row", n_row)
+    states_rows = gather_rows(states, "row", n_row)
+    out_weight_grad = jnp.dot(states_rows, masked, preferred_element_type=jnp.float32).astype(
+        jnp.bfloat16
+    )
     adjoint = adjoint_sweep(state_grad, decay_rate, onehot, seq_count)
     rate_grad = rate_term(adjoint, states, onehot, seq_count)
-    gathered = lax.all_gather(adjoint.astype(jnp.bfloat16), "row", axis=0, tiled=True)
+    gathered = gather_rows(adjoint.astype(jnp.bfloat16), "row", n_row)
+    input_rows = gather_rows(inputs, "col", n_col)
     in_weight_grad = contract(input_rows, gathered, 0, 1).astype(jnp.bfloat16)
-    input_grad = lax.psum_scatter(
-        contract(gathered, in_weight, 0, 1).astype(jnp.bfloat16),
-        "col",
-        scatter_dimension=0,
-        tiled=True,
-    )
+    input_grad = scatter_sum(
+        contract(gathered, in_weight, 0, 1).astype(jnp.bfloat16), "col", n_col
+    ).astype(jnp.bfloat16)
     return (input_grad, in_weight_grad, out_weight_grad, rate_grad)
 
 

time: 525 us -> 290 us (0.55)
  waiting for transfers between devices: 382 us -> 177 us
  local copies, waits for them, and re-layouts: 86.1 us -> 16.4 us
  starting transfers between devices: 0.24 us -> 32.2 us
  blocking collectives: 0 us -> 30.8 us
  between operations: 14.9 us -> 0.89 us
    all_gather x4 -> x0, waiting for transfers between devices: 237 us -> none  [the longest x1 76.5 us: per_device(): lax.all_gather(out_grad, 'col', axis=0, tiled=True)]
    all_to_all x0 -> x5, waiting for transfers between devices: none -> 177 us  [the longest x3 121 us: gather_rows(): lax.all_to_all(spread, axis_name, 0, 0).reshape((-1,) + share.shape[1:])]
    unnamed x7 -> x0, waiting for transfers between devices: 77.2 us -> none
    reduce_scatter x1 -> x0, waiting for transfers between devices: 67.6 us -> none  [per_device(): lax.psum_scatter(contract(gathered, in_weight, 0, 1).astype(jnp.bfloat16)...]
    slice x45 -> x8, local copies, waits for them, and re-layouts: 42 us -> 1.39 us  [adjoint_sweep(): running[:, :, shift:]]
    all_to_all x0 -> x5, starting transfers between devices: none -> 32.2 us  [the longest x3 19.5 us: gather_rows(): lax.all_to_all(spread, axis_name, 0, 0).reshape((-1,) + share.shape[1:])]
    all_to_all x0 -> x1, blocking collectives: none -> 30.8 us  [gather_rows(): lax.all_to_all(spread, axis_name, 0, 0).reshape((-1,) + share.shape[1:])]
    pad x14 -> x0, local copies, waits for them, and re-layouts: 25.1 us -> none  [adjoint_sweep(): lax.associative_scan(combine, (jnp.flip(factor, 2), jnp.flip(grad_seq, 2)...]
  transfers between devices with their start and end apart: 6 -> 5, of which waited for: 6 -> 5; matrix products, arithmetic and copies ran while one was open for 5% -> 12% of each run, Pallas kernels for 0% -> 0%
where the time goes in v1:
time: 290 us; the launch traced here: 289 us
  waiting for transfers between devices  177 us (61%)
  starting transfers between devices  32.2 us (11%)
  blocking collectives  30.8 us (11%)
  matrix products  21.9 us (8%)
  local copies, waits for them, and re-layouts  16.4 us (6%)
  other arithmetic  9.85 us (3%)
    all_to_all x3, waiting for transfers between devices, gather_rows(): lax.all_to_all(spread, axis_name, 0, 0).reshape((-1,) + share.shape[1:])  121 us
    all_to_all x2, waiting for transfers between devices, scatter_sum(): lax.all_to_all(partial.reshape((parts, -1) + partial.shape[1:]), axis_nam...  56 us
    all_to_all x1, blocking collectives, gather_rows(): lax.all_to_all(spread, axis_name, 0, 0).reshape((-1,) + share.shape[1:])  30.8 us
    all_to_all x3, starting transfers between devices, gather_rows(): lax.all_to_all(spread, axis_name, 0, 0).reshape((-1,) + share.shape[1:])  19.5 us
    dot_general x3, matrix products, contract(): lax.dot_general(left_side, right_side, (((left_dim,), (right_dim,)), ((),...  15.5 us
    all_to_all x2, starting transfers between devices, scatter_sum(): lax.all_to_all(partial.reshape((parts, -1) + partial.shape[1:]), axis_nam...  12.8 us
    unnamed x15, local copies, waits for them, and re-layouts  7.91 us
    broadcast_in_dim x4, local copies, waits for them, and re-layouts, gather_rows(): spread = jnp.broadcast_to(share[None], (parts,) + share.shape)  6.05 us
  transfers between devices with their start and end apart: 5, of which 5 were waited for; matrix products, arithmetic and copies ran while one was open for 12% of the time, Pallas kernels for 0%

profile of v1, /device:TPU:2, one launch (start us, length us, event | category | flops | bytes accessed | tf_op | source)
XLA Modules:
  0.0 288.9 jit_solution(3348150130496277099)
XLA Ops:
  0.6 0.0 copy-start
  0.6 2.6 broadcast_in_dim.37
  3.3 0.0 copy-start.3
  3.3 9.8 %all-to-all-start = ((bf16[16,64,1024]{2,1,0:T(8,128)(2,1)}), bf16[16,64,1024]{2,1,0:T(8,128)(2,1)}, u32[]{:S(2)}, u32[]{:S(2)}) async-start(bf16[16,64,1024]{2,1,0:T(8,128)(2,1)} %broadcast_in_dim.37), calls=%async_computation | async-start | bytes 4194304 | tf_op jit(solution)/shard_map/all_to_all | solution.py:26
  13.1 0.0 copy-done.3
  13.1 0.1 select_reduce_fusion
  13.2 50.4 %all-to-all-done = bf16[16,64,1024]{2,1,0:T(8,128)(2,1)} async-done(((bf16[16,64,1024]{2,1,0:T(8,128)(2,1)}), bf16[16,64,1024]{2,1,0:T(8,128)(2,1)}, u32[]{:S(2)}, u32[]{:S(2)}) %all-to-all-start) | async-done | bytes 2097184 | tf_op jit(solution)/shard_map/all_to_all | solution.py:26
  63.6 1.8 bitcast_select_fusion
  65.4 0.0 copy-done
  65.4 3.7 %convolution_convert_fusion.1 = bf16[1024,1024]{0,1:T(8,128)(2,1)} fusion(bf16[1024,1024]{1,0:T(8,128)(2,1)S(1)} %bitcast_select_fusion, bf16[1024,1024]{1,0:T(8,128)(2,1)S(1)} %copy-done), kind=kOutput, calls=%fused_computation.6 | convolution fusion | flops 2148532224 | bytes 6291456 | tf_op jit(solution)/shard_map/dot_general | solution.py:10
  69.1 7.3 %all-to-all-start.1 = ((bf16[16,64,1024]{2,1,0:T(8,128)(2,1)}), bf16[16,64,1024]{2,1,0:T(8,128)(2,1)}, u32[]{:S(2)}, u32[]{:S(2)}) async-start(bf16[16,64,1024]{2,1,0:T(8,128)(2,1)} %bitcast.31), calls=%async_computation.1 | async-start | bytes 4194304 | tf_op jit(solution)/shard_map/all_to_all | solution.py:30
  76.5 0.0 copy-done.4
  76.5 0.0 copy-done.5
  76.5 0.2 multiply_multiply_fusion
  76.7 0.1 copy.22
  76.8 0.1 copy.23
  76.9 0.1 copy.24
  77.0 0.1 copy.25
  77.0 0.1 copy.26
  77.1 0.1 copy.27
  77.2 0.1 copy.28
  77.3 0.1 copy.29
  77.4 27.7 %all-to-all-done.1 = bf16[16,64,1024]{2,1,0:T(8,128)(2,1)} async-done(((bf16[16,64,1024]{2,1,0:T(8,128)(2,1)}), bf16[16,64,1024]{2,1,0:T(8,128)(2,1)}, u32[]{:S(2)}, u32[]{:S(2)}) %all-to-all-start.1) | async-done | bytes 2097184 | tf_op jit(solution)/shard_map/all_to_all | solution.py:30
  105.1 0.0 copy-done.1
  105.1 1.6 broadcast_in_dim.43
  106.7 5.2 %all-to-all-start.5 = ((bf16[16,64,1024]{2,1,0:T(8,128)(2,1)}), bf16[16,64,1024]{2,1,0:T(8,128)(2,1)}, u32[]{:S(2)}, u32[]{:S(2)}) async-start(bf16[16,64,1024]{2,1,0:T(8,128)(2,1)} %broadcast_in_dim.43), calls=%async_computation.5 | async-start | bytes 4194304 | tf_op jit(solution)/shard_map/all_to_all | solution.py:26
  111.9 2.0 convert_reduce_fusion
  113.9 0.1 reshape.98
  114.1 0.2 slice.44
  114.3 0.1 multiply_add_fusion.7
  114.4 0.2 slice.45
  114.6 0.1 multiply_add_fusion.6
  114.8 0.2 slice.46
  115.0 0.1 multiply_add_fusion.5
  115.1 0.2 slice.47
  115.3 0.1 multiply_add_fusion.4
  115.5 0.2 slice.48
  115.7 0.1 multiply_add_fusion.3
  115.8 0.2 slice.49
  116.0 0.1 multiply_add_fusion.2
  116.2 0.2 slice.50
  116.4 0.1 multiply_add_fusion.1
  116.5 0.1 fusion.18
  116.7 23.8 %all-to-all-done.5 = bf16[16,64,1024]{2,1,0:T(8,128)(2,1)} async-done(((bf16[16,64,1024]{2,1,0:T(8,128)(2,1)}), bf16[16,64,1024]{2,1,0:T(8,128)(2,1)}, u32[]{:S(2)}, u32[]{:S(2)}) %all-to-all-start.5) | async-done | bytes 2097184 | tf_op jit(solution)/shard_map/all_to_all | solution.py:26
  140.6 0.3 broadcast_in_dim.39
  140.8 0.0 copy-start.2
  140.8 30.8 %all_to_all.30 = bf16[16,64,1024]{2,1,0:T(8,128)(2,1)} all-to-all(bf16[16,64,1024]{2,1,0:T(8,128)(2,1)S(1)} %broadcast_in_dim.39), channel_id=1, replica_groups=mesh['row'=16,'col'=16] {'row'}, dimensions={0} | all-to-all | bytes 4194304 | tf_op jit(solution)/shard_map/all_to_all | solution.py:26
  171.6 0.0 copy-done.2
  171.6 1.6 broadcast_in_dim.40
  173.2 4.5 %all-to-all-start.4 = ((bf16[16,64,1024]{2,1,0:T(8,128)(2,1)}), bf16[16,64,1024]{2,1,0:T(8,128)(2,1)}, u32[]{:S(2)}, u32[]{:S(2)}) async-start(bf16[16,64,1024]{2,1,0:T(8,128)(2,1)} %broadcast_in_dim.40), calls=%async_computation.4 | async-start | bytes 4194304 | tf_op jit(solution)/shard_map/all_to_all | solution.py:26
  177.6 5.9 %convolution_convert_fusion = bf16[1024,1024]{1,0:T(8,128)(2,1)} fusion(bf16[1024,1024]{1,0:T(8,128)(2,1)} %bitcast.28, bf16[1024,1024]{1,0:T(8,128)(2,1)} %param.11), kind=kOutput, calls=%fused_computation.5 | convolution fusion | flops 2148532224 | bytes 6291456 | tf_op jit(solution)/shard_map/dot_general | solution.py:10
  183.6 46.6 %all-to-all-done.4 = bf16[16,64,1024]{2,1,0:T(8,128)(2,1)} async-done(((bf16[16,64,1024]{2,1,0:T(8,128)(2,1)}), bf16[16,64,1024]{2,1,0:T(8,128)(2,1)}, u32[]{:S(2)}, u32[]{:S(2)}) %all-to-all-start.4) | async-done | bytes 2097184 | tf_op jit(solution)/shard_map/all_to_all | solution.py:26
  230.2 5.5 %all-to-all-start.3 = ((bf16[16,64,1024]{2,1,0:T(8,128)(2,1)}), bf16[16,64,1024]{2,1,0:T(8,128)(2,1)}, u32[]{:S(2)}, u32[]{:S(2)}) async-start(bf16[16,64,1024]{2,1,0:T(8,128)(2,1)} %bitcast.30), calls=%async_computation.3 | async-start | bytes 4194304 | tf_op jit(solution)/shard_map/all_to_all | solution.py:30
  235.7 0.1 reshape.103
  235.7 0.1 sub.33
  235.8 1.8 broadcast_select_fusion
  237.6 5.3 %convert_bitcast_fusion = bf16[1024,1024]{0,1:T(8,128)(2,1)} fusion(bf16[1024,1024]{1,0:T(8,128)(2,1)S(1)} %bitcast.32, bf16[1024,1024]{1,0:T(8,128)(2,1)} %bitcast.9), kind=kOutput, calls=%fused_computation.2 | convolution fusion | flops 2148532224 | bytes 6291456 | tf_op jit(solution)/shard_map/dot_general | solution.py:75
  243.0 3.9 %copy.31 = bf16[1024,1024]{1,0:T(8,128)(2,1)} copy(bf16[1024,1024]{0,1:T(8,128)(2,1)} %convert_bitcast_fusion) | data formatting | bytes 4194304
  246.9 0.3 fusion.1
  247.2 0.9 convolution_negate_fusion
  248.0 5.9 %convert_bitcast_fusion.1 = bf16[1024,1024]{0,1:T(8,128)(2,1)} fusion(bf16[1024,1024]{1,0:T(8,128)(2,1)} %bitcast.29, bf16[1024,1024]{1,0:T(8,128)(2,1)} %bitcast.6), kind=kOutput, calls=%fused_computation.3 | convolution fusion | flops 2148532224 | bytes 6291456 | tf_op jit(solution)/shard_map/dot_general | solution.py:10
  253.9 3.9 %copy.30 = bf16[1024,1024]{1,0:T(8,128)(2,1)} copy(bf16[1024,1024]{0,1:T(8,128)(2,1)} %convert_bitcast_fusion.1) | data formatting | bytes 4194304
  257.9 28.3 %all-to-all-done.3 = bf16[16,64,1024]{2,1,0:T(8,128)(2,1)} async-done(((bf16[16,64,1024]{2,1,0:T(8,128)(2,1)}), bf16[16,64,1024]{2,1,0:T(8,128)(2,1)}, u32[]{:S(2)}, u32[]{:S(2)}) %all-to-all-start.3) | async-done | bytes 2097184 | tf_op jit(solution)/shard_map/all_to_all | solution.py:30
  286.2 2.7 reduce_sum.41
  (9 shorter events, 0.1 us)
Async XLA Ops:
  0.6 64.8 %copy-start = (bf16[1024,1024]{1,0:T(8,128)(2,1)S(1)}, bf16[1024,1024]{1,0:T(8,128)(2,1)}, u32[]{:S(2)}) copy-start(bf16[1024,1024]{1,0:T(8,128)(2,1)} %param.12) | copy-start | bytes 6291460
  3.3 9.8 %copy-start.3 = (s32[4]{0:T(128)S(1)}, s32[4]{0:T(128)}, u32[]{:S(2)}) copy-start(s32[4]{0:T(128)} %param.15) | copy-start | bytes 52
  3.3 60.3 %all-to-all-start = ((bf16[16,64,1024]{2,1,0:T(8,128)(2,1)}), bf16[16,64,1024]{2,1,0:T(8,128)(2,1)}, u32[]{:S(2)}, u32[]{:S(2)}) async-start(bf16[16,64,1024]{2,1,0:T(8,128)(2,1)} %broadcast_in_dim.37), calls=%async_computation | async-start | bytes 4194304 | tf_op jit(solution)/shard_map/all_to_all | solution.py:26
  69.1 7.3 %copy-start.4 = (f32[4,64]{1,0:T(4,128)S(1)}, f32[4,64]{1,0:T(4,128)}, u32[]{:S(2)}) copy-start(f32[4,64]{1,0:T(4,128)} %param.13) | copy-start | bytes 3076
  69.1 7.3 %copy-start.5 = (s32[4]{0:T(128)S(1)}, s32[4]{0:T(128)}, u32[]{:S(2)}) copy-start(s32[4]{0:T(128)} %param.14) | copy-start | bytes 52
  69.1 36.0 %copy-start.1 = (bf16[64,1024]{1,0:T(8,128)(2,1)S(1)}, bf16[64,1024]{1,0:T(8,128)(2,1)}, u32[]{:S(2)}) copy-start(bf16[64,1024]{1,0:T(8,128)(2,1)} %param.10) | copy-start | bytes 393220
  69.1 36.0 %all-to-all-start.1 = ((bf16[16,64,1024]{2,1,0:T(8,128)(2,1)}), bf16[16,64,1024]{2,1,0:T(8,128)(2,1)}, u32[]{:S(2)}, u32[]{:S(2)}) async-start(bf16[16,64,1024]{2,1,0:T(8,128)(2,1)} %bitcast.31), calls=%async_computation.1 | async-start | bytes 4194304 | tf_op jit(solution)/shard_map/all_to_all | solution.py:30
  106.7 33.9 %all-to-all-start.5 = ((bf16[16,64,1024]{2,1,0:T(8,128)(2,1)}), bf16[16,64,1024]{2,1,0:T(8,128)(2,1)}, u32[]{:S(2)}, u32[]{:S(2)}) async-start(bf16[16,64,1024]{2,1,0:T(8,128)(2,1)} %broadcast_in_dim.43), calls=%async_computation.5 | async-start | bytes 4194304 | tf_op jit(solution)/shard_map/all_to_all | solution.py:26
  140.8 30.8 %copy-start.2 = (bf16[64,1024]{1,0:T(8,128)(2,1)S(1)}, bf16[64,1024]{1,0:T(8,128)(2,1)}, u32[]{:S(2)}) copy-start(bf16[64,1024]{1,0:T(8,128)(2,1)} %param.8) | copy-start | bytes 393220
  173.2 57.0 %all-to-all-start.4 = ((bf16[16,64,1024]{2,1,0:T(8,128)(2,1)}), bf16[16,64,1024]{2,1,0:T(8,128)(2,1)}, u32[]{:S(2)}, u32[]{:S(2)}) async-start(bf16[16,64,1024]{2,1,0:T(8,128)(2,1)} %broadcast_in_dim.40), calls=%async_computation.4 | async-start | bytes 4194304 | tf_op jit(solution)/shard_map/all_to_all | solution.py:26
  230.2 56.0 %all-to-all-start.3 = ((bf16[16,64,1024]{2,1,0:T(8,128)(2,1)}), bf16[16,64,1024]{2,1,0:T(8,128)(2,1)}, u32[]{:S(2)}, u32[]{:S(2)}) async-start(bf16[16,64,1024]{2,1,0:T(8,128)(2,1)} %bitcast.30), calls=%async_computation.3 | async-start | bytes 4194304 | tf_op jit(solution)/shard_map/all_to_all | solution.py:30

commit v2 on v1

--- a/solution.py
+++ b/solution.py
@@ -71,14 +71,14 @@
     valid_bin = token_ids % bin_count >= bin_count - seq_length
     masked = jnp.where(valid_bin[:, None], grad_rows, jnp.zeros_like(grad_rows))
     state_grad = scatter_sum(contract(out_weight, masked, 1, 1).astype(jnp.bfloat16), "row", n_row)
-    states_rows = gather_rows(states, "row", n_row)
+    states_rows = lax.all_gather(states, "row", axis=0, tiled=True)
     out_weight_grad = jnp.dot(states_rows, masked, preferred_element_type=jnp.float32).astype(
         jnp.bfloat16
     )
     adjoint = adjoint_sweep(state_grad, decay_rate, onehot, seq_count)
     rate_grad = rate_term(adjoint, states, onehot, seq_count)
     gathered = gather_rows(adjoint.astype(jnp.bfloat16), "row", n_row)
-    input_rows = gather_rows(inputs, "col", n_col)
+    input_rows = lax.all_gather(inputs, "col", axis=0, tiled=True)
     in_weight_grad = contract(input_rows, gathered, 0, 1).astype(jnp.bfloat16)
     input_grad = scatter_sum(
         contract(gathered, in_weight, 0, 1).astype(jnp.bfloat16), "col", n_col

time: 290 us -> 285 us (0.983)
  blocking collectives: 30.8 us -> 0 us
  waiting for transfers between devices: 177 us -> 197 us
  between operations: 0.89 us -> 14.3 us
  starting transfers between devices: 32.2 us -> 27.6 us
    all_gather x0 -> x2, waiting for transfers between devices: none -> 87.4 us  [the longest x1 87.4 us: per_device(): input_rows = lax.all_gather(inputs, 'col', axis=0, tiled=True)]
    all_to_all x3 -> x2, waiting for transfers between devices: 121 us -> 80.5 us  [gather_rows(): lax.all_to_all(spread, axis_name, 0, 0).reshape((-1,) + share.shape[1:])]
    all_to_all x1 -> x0, blocking collectives: 30.8 us -> none  [gather_rows(): lax.all_to_all(spread, axis_name, 0, 0).reshape((-1,) + share.shape[1:])]
    all_to_all x2, waiting for transfers between devices: 56 us -> 28.2 us  [scatter_sum(): lax.all_to_all(partial.reshape((parts, -1) + partial.shape[1:]), axis_nam...]
    all_to_all x3 -> x2, starting transfers between devices: 19.5 us -> 15.5 us  [gather_rows(): lax.all_to_all(spread, axis_name, 0, 0).reshape((-1,) + share.shape[1:])]
    broadcast_in_dim x4 -> x2, local copies, waits for them, and re-layouts: 6.05 us -> 4.21 us  [gather_rows(): spread = jnp.broadcast_to(share[None], (parts,) + share.shape)]
  transfers between devices with their start and end apart: 5 -> 6, of which waited for: 5 -> 4; matrix products, arithmetic and copies ran while one was open for 12% -> 12% of each run, Pallas kernels for 0% -> 0%
where the time goes in v2:
time: 285 us; the launch traced here: 284 us
  waiting for transfers between devices  197 us (69%)
  starting transfers between devices  27.6 us (10%)
  matrix products  22.5 us (8%)
  local copies, waits for them, and re-layouts  14.5 us (5%)
  between operations  14.3 us (5%)
  other arithmetic  8.02 us (3%)
    all_gather x1, waiting for transfers between devices, per_device(): input_rows = lax.all_gather(inputs, 'col', axis=0, tiled=True)  87.4 us
    all_to_all x2, waiting for transfers between devices, gather_rows(): lax.all_to_all(spread, axis_name, 0, 0).reshape((-1,) + share.shape[1:])  80.5 us
    all_to_all x2, waiting for transfers between devices, scatter_sum(): lax.all_to_all(partial.reshape((parts, -1) + partial.shape[1:]), axis_nam...  28.2 us
    dot_general x3, matrix products, contract(): lax.dot_general(left_side, right_side, (((left_dim,), (right_dim,)), ((),...  15.5 us
    all_to_all x2, starting transfers between devices, gather_rows(): lax.all_to_all(spread, axis_name, 0, 0).reshape((-1,) + share.shape[1:])  15.5 us
    all_to_all x2, starting transfers between devices, scatter_sum(): lax.all_to_all(partial.reshape((parts, -1) + partial.shape[1:]), axis_nam...  12.1 us
    unnamed x15, local copies, waits for them, and re-layouts  7.91 us
    dot_general x1, matrix products, per_device(): jnp.dot(states_rows, masked, preferred_element_type=jnp.float32)  5.94 us
  transfers between devices with their start and end apart: 6, of which 4 were waited for; matrix products, arithmetic and copies ran while one was open for 12% of the time, Pallas kernels for 0%

profile of v2, /device:TPU:2, one launch (start us, length us, event | category | flops | bytes accessed | tf_op | source)
XLA Modules:
  0.0 284.3 jit_solution(6921144148416662720)
XLA Ops:
  7.2 0.0 copy-start
  7.2 2.6 broadcast_in_dim.26
  9.8 0.0 copy-start.3
  9.8 9.8 %all-to-all-start = ((bf16[16,64,1024]{2,1,0:T(8,128)(2,1)}), bf16[16,64,1024]{2,1,0:T(8,128)(2,1)}, u32[]{:S(2)}, u32[]{:S(2)}) async-start(bf16[16,64,1024]{2,1,0:T(8,128)(2,1)} %broadcast_in_dim.26), calls=%async_computation | async-start | bytes 4194304 | tf_op jit(solution)/shard_map/all_to_all | solution.py:26
  19.6 0.0 copy-done.3
  19.6 0.1 select_reduce_fusion
  19.7 50.4 %all-to-all-done = bf16[16,64,1024]{2,1,0:T(8,128)(2,1)} async-done(((bf16[16,64,1024]{2,1,0:T(8,128)(2,1)}), bf16[16,64,1024]{2,1,0:T(8,128)(2,1)}, u32[]{:S(2)}, u32[]{:S(2)}) %all-to-all-start) | async-done | bytes 2097184 | tf_op jit(solution)/shard_map/all_to_all | solution.py:26
  70.1 1.8 bitcast_select_fusion
  72.0 0.0 copy-done
  72.0 0.0 copy-start.1
  72.0 3.7 %convolution_convert_fusion.1 = bf16[1024,1024]{0,1:T(8,128)(2,1)} fusion(bf16[1024,1024]{1,0:T(8,128)(2,1)S(1)} %bitcast_select_fusion, bf16[1024,1024]{1,0:T(8,128)(2,1)S(1)} %copy-done), kind=kOutput, calls=%fused_computation.5 | convolution fusion | flops 2148532224 | bytes 6291456 | tf_op jit(solution)/shard_map/dot_general | solution.py:10
  75.7 0.0 copy-done.1
  75.7 0.0 copy-start.4
  75.7 7.3 %all-to-all-start.1 = ((bf16[16,64,1024]{2,1,0:T(8,128)(2,1)}), bf16[16,64,1024]{2,1,0:T(8,128)(2,1)}, u32[]{:S(2)}, u32[]{:S(2)}) async-start(bf16[16,64,1024]{2,1,0:T(8,128)(2,1)} %bitcast.25), calls=%async_computation.1 | async-start | bytes 4194304 | tf_op jit(solution)/shard_map/all_to_all | solution.py:30
  83.0 0.0 all-gather.5.cloned.1.call-start
  83.1 0.7 all-gather.5.cloned.1.call-update
  83.7 0.0 copy-done.4
  83.8 0.0 copy-done.5
  83.8 0.2 multiply_multiply_fusion
  84.0 0.1 copy.22
  84.1 0.1 copy.23
  84.1 0.1 copy.24
  84.2 0.1 copy.25
  84.3 0.1 copy.26
  84.4 0.1 copy.27
  84.5 0.1 copy.28
  84.6 0.1 copy.29
  84.7 28.2 %all-to-all-done.1 = bf16[16,64,1024]{2,1,0:T(8,128)(2,1)} async-done(((bf16[16,64,1024]{2,1,0:T(8,128)(2,1)}), bf16[16,64,1024]{2,1,0:T(8,128)(2,1)}, u32[]{:S(2)}, u32[]{:S(2)}) %all-to-all-start.1) | async-done | bytes 2097184 | tf_op jit(solution)/shard_map/all_to_all | solution.py:30
  112.9 2.0 convert_reduce_fusion
  114.9 0.1 reshape.80
  115.0 0.2 slice.44
  115.2 0.2 multiply_add_fusion.7
  115.4 0.2 slice.45
  115.6 0.1 multiply_add_fusion.6
  115.7 0.2 slice.46
  115.9 0.1 multiply_add_fusion.5
  116.1 0.2 slice.47
  116.3 0.1 multiply_add_fusion.4
  116.4 0.2 slice.48
  116.6 0.1 multiply_add_fusion.3
  116.8 0.2 slice.49
  117.0 0.1 multiply_add_fusion.2
  117.1 0.2 slice.50
  117.3 0.1 multiply_add_fusion.1
  117.5 0.1 fusion.14
  117.7 1.6 broadcast_in_dim.28
  119.3 5.7 %all-to-all-start.2 = ((bf16[16,64,1024]{2,1,0:T(8,128)(2,1)}), bf16[16,64,1024]{2,1,0:T(8,128)(2,1)}, u32[]{:S(2)}, u32[]{:S(2)}) async-start(bf16[16,64,1024]{2,1,0:T(8,128)(2,1)} %broadcast_in_dim.28), calls=%async_computation.2 | async-start | bytes 4194304 | tf_op jit(solution)/shard_map/all_to_all | solution.py:26
  125.0 0.0 all-gather.3.cloned.1.call-start
  125.0 0.7 all-gather.3.cloned.1.call-update
  125.7 30.0 %all-to-all-done.2 = bf16[16,64,1024]{2,1,0:T(8,128)(2,1)} async-done(((bf16[16,64,1024]{2,1,0:T(8,128)(2,1)}), bf16[16,64,1024]{2,1,0:T(8,128)(2,1)}, u32[]{:S(2)}, u32[]{:S(2)}) %all-to-all-start.2) | async-done | bytes 2097184 | tf_op jit(solution)/shard_map/all_to_all | solution.py:26
  155.7 5.9 %convolution_convert_fusion = bf16[1024,1024]{1,0:T(8,128)(2,1)} fusion(bf16[1024,1024]{1,0:T(8,128)(2,1)} %bitcast.4, bf16[1024,1024]{1,0:T(8,128)(2,1)} %param.11), kind=kOutput, calls=%fused_computation.4 | convolution fusion | flops 2148532224 | bytes 6291456 | tf_op jit(solution)/shard_map/dot_general | solution.py:10
  161.7 4.7 %all-to-all-start.3 = ((bf16[16,64,1024]{2,1,0:T(8,128)(2,1)}), bf16[16,64,1024]{2,1,0:T(8,128)(2,1)}, u32[]{:S(2)}, u32[]{:S(2)}) async-start(bf16[16,64,1024]{2,1,0:T(8,128)(2,1)} %bitcast.26), calls=%async_computation.3 | async-start | bytes 4194304 | tf_op jit(solution)/shard_map/all_to_all | solution.py:30
  166.4 0.0 copy-done.2
  166.4 0.1 reshape.83
  166.5 0.0 all-gather.5.cloned.1.call-done
  166.5 5.9 %convert_bitcast_fusion = bf16[1024,1024]{0,1:T(8,128)(2,1)} fusion(bf16[1024,1024]{1,0:T(8,128)(2,1)} %copy-done.1, bf16[1024,1024]{1,0:T(8,128)(2,1)} %all-gather.5.cloned.1.call-done), kind=kOutput, calls=%fused_computation.2 | convolution fusion | flops 2148532224 | bytes 6291456 | tf_op jit(solution)/shard_map/dot_general | solution.py:75
  172.5 3.9 %copy.31 = bf16[1024,1024]{1,0:T(8,128)(2,1)} copy(bf16[1024,1024]{0,1:T(8,128)(2,1)} %convert_bitcast_fusion) | data formatting | bytes 4194304
  176.4 0.3 fusion.1
  176.7 0.9 convolution_negate_fusion
  177.6 87.4 %all-gather.3.cloned.1.call-done = bf16[1024,1024]{1,0:T(8,128)(2,1)} async-done(((bf16[64,1024]{1,0:T(8,128)(2,1)}), bf16[1024,1024]{1,0:T(8,128)(2,1)}) %all-gather.3.cloned.1.call-update) | async-done | bytes 2097168 | tf_op jit(solution)/shard_map/all_gather | solution.py:81
  265.0 5.9 %convert_bitcast_fusion.1 = bf16[1024,1024]{0,1:T(8,128)(2,1)} fusion(bf16[1024,1024]{1,0:T(8,128)(2,1)} %bitcast.4, bf16[1024,1024]{1,0:T(8,128)(2,1)} %all-gather.3.cloned.1.call-done), kind=kOutput, calls=%fused_computation.3 | convolution fusion | flops 2148532224 | bytes 6291456 | tf_op jit(solution)/shard_map/dot_general | solution.py:10
  270.9 3.9 %copy.30 = bf16[1024,1024]{1,0:T(8,128)(2,1)} copy(bf16[1024,1024]{0,1:T(8,128)(2,1)} %convert_bitcast_fusion.1) | data formatting | bytes 4194304
  274.8 0.0 all-to-all-done.3
  274.8 2.7 reduce_sum.41
  (6 shorter events, 0.1 us)
Async XLA Ops:
  7.2 64.8 %copy-start = (bf16[1024,1024]{1,0:T(8,128)(2,1)S(1)}, bf16[1024,1024]{1,0:T(8,128)(2,1)}, u32[]{:S(2)}) copy-start(bf16[1024,1024]{1,0:T(8,128)(2,1)} %param.12) | copy-start | bytes 6291460
  9.8 9.8 %copy-start.3 = (s32[4]{0:T(128)S(1)}, s32[4]{0:T(128)}, u32[]{:S(2)}) copy-start(s32[4]{0:T(128)} %param.15) | copy-start | bytes 52
  9.8 60.3 %all-to-all-start = ((bf16[16,64,1024]{2,1,0:T(8,128)(2,1)}), bf16[16,64,1024]{2,1,0:T(8,128)(2,1)}, u32[]{:S(2)}, u32[]{:S(2)}) async-start(bf16[16,64,1024]{2,1,0:T(8,128)(2,1)} %broadcast_in_dim.26), calls=%async_computation | async-start | bytes 4194304 | tf_op jit(solution)/shard_map/all_to_all | solution.py:26
  72.0 3.7 %copy-start.1 = (bf16[1024,1024]{1,0:T(8,128)(2,1)}, bf16[1024,1024]{1,0:T(8,128)(2,1)S(1)}, u32[]{:S(2)}) copy-start(bf16[1024,1024]{1,0:T(8,128)(2,1)S(1)} %bitcast_select_fusion) | copy-start | bytes 6291460
  75.7 8.1 %copy-start.4 = (f32[4,64]{1,0:T(4,128)S(1)}, f32[4,64]{1,0:T(4,128)}, u32[]{:S(2)}) copy-start(f32[4,64]{1,0:T(4,128)} %param.13) | copy-start | bytes 3076
  75.7 8.1 %copy-start.5 = (s32[4]{0:T(128)S(1)}, s32[4]{0:T(128)}, u32[]{:S(2)}) copy-start(s32[4]{0:T(128)} %param.14) | copy-start | bytes 52
  75.7 37.2 %all-to-all-start.1 = ((bf16[16,64,1024]{2,1,0:T(8,128)(2,1)}), bf16[16,64,1024]{2,1,0:T(8,128)(2,1)}, u32[]{:S(2)}, u32[]{:S(2)}) async-start(bf16[16,64,1024]{2,1,0:T(8,128)(2,1)} %bitcast.25), calls=%async_computation.1 | async-start | bytes 4194304 | tf_op jit(solution)/shard_map/all_to_all | solution.py:30
  83.0 83.5 %all-gather.5.cloned.1.call-start = ((), (), s32[]{:S(2)}) async-start(), calls=%async_computation.5 | async-start | bytes 2228224 | tf_op jit(solution)/shard_map/all_gather | solution.py:74
  119.3 36.5 %all-to-all-start.2 = ((bf16[16,64,1024]{2,1,0:T(8,128)(2,1)}), bf16[16,64,1024]{2,1,0:T(8,128)(2,1)}, u32[]{:S(2)}, u32[]{:S(2)}) async-start(bf16[16,64,1024]{2,1,0:T(8,128)(2,1)} %broadcast_in_dim.28), calls=%async_computation.2 | async-start | bytes 4194304 | tf_op jit(solution)/shard_map/all_to_all | solution.py:26
  125.0 140.0 %all-gather.3.cloned.1.call-start = ((), (), s32[]{:S(2)}) async-start(), calls=%async_computation.4 | async-start | bytes 2228224 | tf_op jit(solution)/shard_map/all_gather | solution.py:81
  161.7 4.8 %copy-start.2 = (bf16[64,1024]{1,0:T(8,128)(2,1)S(1)}, bf16[64,1024]{1,0:T(8,128)(2,1)}, u32[]{:S(2)}) copy-start(bf16[64,1024]{1,0:T(8,128)(2,1)} %param.10) | copy-start | bytes 393220
  161.7 113.1 %all-to-all-start.3 = ((bf16[16,64,1024]{2,1,0:T(8,128)(2,1)}), bf16[16,64,1024]{2,1,0:T(8,128)(2,1)}, u32[]{:S(2)}, u32[]{:S(2)}) async-start(bf16[16,64,1024]{2,1,0:T(8,128)(2,1)} %bitcast.26), calls=%async_computation.3 | async-start | bytes 4194304 | tf_op jit(solution)/shard_map/all_to_all | solution.py:30
Sparse Core Ops, SparseCore 0:
  86.5 76.7 all-gather.4
  165.2 99.7 all-gather.2
